TPU v7x, 512 devices: a whole 4x4x16 slice. The times are simulated.
512 devices in a mesh: rep: 32 (over z_lo, x), seq: 16 (over z_hi, y, core).
Axes of the slice: x: 4, y: 4, z: 16 (z_hi: 2, z_lo: 8; z = z_hi * 8 + z_lo), core: 2. Of those that a mesh axis runs over, the one named last changes fastest.
Arguments:
- tokens: bfloat16 [32, 4096, 6144], P('rep', 'seq'), may hold values from -6 to 6
- queries: bfloat16 [32, 4096, 128], P('rep', 'seq'), may hold values from -4 to 4
- ctx_grad: bfloat16 [32, 4096, 128], P('rep', 'seq'), may hold values from -0.25 to 0.25
- kv_weight: bfloat16 [32, 6144, 256], P('rep', 'seq'), may hold values from -0.078125 to 0.078125
- rand_blocks: int32 [64, 3], replicated, may hold values from 0 to 63
- step_count: int32 [1], replicated, may hold values from 0 to 63
Outputs:
- mixed_update: float32 [32, 6144, 256], P('rep', 'seq')
- query_grad: bfloat16 [32, 4096, 128], P('rep', 'seq')
Inputs may be any that keep to these rules, and one draw needn't show every extreme that they name: `rand_blocks`: block indices of the same replica sequence.
All inputs are finite; a program needn't handle non-finite values.
Results may differ from a plain program's by a relative error of at most 0.02.
Values may be sent and summed in bfloat16 or wider, within the bound.
No kernel may reach another device: no remote copies, remote signals or barrier semaphores. Data moves between devices by JAX's collectives and lax.ppermute only.
A program may use at most 64 MiB of HBM per device.

v0:
```python
from functools import partial
import jax
import jax.numpy as jnp
from jax import lax
from jax.sharding import PartitionSpec as P

BLOCK = 64


def for_sending(value):

    def short(part):
        return part.astype(jnp.bfloat16) if part.dtype == jnp.float32 else part

    return jax.tree.map(short, value)


def shifted(value, axis, steps):
    count = lax.axis_size(axis)
    pairs = [(source, (source + steps) % count) for source in range(count)]
    return lax.ppermute(value, axis, pairs)


def fold_rows(tok_rows, row_piece):
    return jnp.dot(tok_rows, row_piece, preferred_element_type=jnp.float32)


def contract_rows(matrix_a, matrix_b):
    return lax.dot_general(
        matrix_a, matrix_b, (((0,), (0,)), ((), ())), preferred_element_type=jnp.float32
    )


def contract_cols(matrix_a, matrix_b):
    return lax.dot_general(
        matrix_a, matrix_b, (((1,), (1,)), ((), ())), preferred_element_type=jnp.float32
    )


def attend_mask(query_blocks, key_blocks, chosen_rows, blk_size):
    is_near = jnp.abs(query_blocks[:, None] - key_blocks[None, :]) <= 1
    picked = jnp.any(chosen_rows[:, :, None] == key_blocks[None, None, :], axis=1)
    allowed = is_near | (key_blocks[None, :] == 0) | picked
    return jnp.repeat(jnp.repeat(allowed, blk_size, axis=0), blk_size, axis=1)


def gossip(update, distance, rep_count):
    if distance == 0:
        return update
    from_low = jax.tree.map(
        lambda part, own: part.astype(own.dtype),
        shifted(for_sending(update), "rep", distance),
        update,
    )
    from_high = jax.tree.map(
        lambda part, own: part.astype(own.dtype),
        shifted(for_sending(update), "rep", rep_count - distance),
        update,
    )
    return (update + from_low + from_high) / 3.0


def per_device(tokens, queries, ctx_grad, kv_weight, rand_blocks, step_count):
    tokens_here = tokens[0]
    query_here = queries[0]
    grad_here = ctx_grad[0]
    weight_here = kv_weight[0]
    seq_count = lax.axis_size("seq")
    rep_count = lax.axis_size("rep")
    seq_index = lax.axis_index("seq")
    tok_count = tokens_here.shape[0]
    kv_width = weight_here.shape[1]
    head_size = kv_width // 2
    blk_size = BLOCK
    blocks_dev = tok_count // blk_size
    block_count = blocks_dev * seq_count
    inv_root = head_size ** (-0.5)
    kv_here = fold_rows(tokens_here, lax.all_gather(weight_here, "seq", axis=0, tiled=True)).astype(
        jnp.bfloat16
    )
    kv_all = lax.all_gather(kv_here, "seq", axis=0, tiled=True)
    keys_all = kv_all[:, :head_size]
    values_all = kv_all[:, head_size:]
    blocks_here = seq_index * blocks_dev + jnp.arange(blocks_dev, dtype=jnp.int32)
    every_block = jnp.arange(block_count, dtype=jnp.int32)
    chosen_here = lax.dynamic_slice_in_dim(rand_blocks, seq_index * blocks_dev, blocks_dev, 0)
    allowed = attend_mask(blocks_here, every_block, chosen_here, blk_size)
    scores = contract_cols(query_here, keys_all) * inv_root
    unnorm = jnp.where(allowed, jnp.exp(scores), jnp.float32(0.0))
    row_total = jnp.sum(unnorm, axis=1, keepdims=True)
    prob_rows = unnorm / row_total
    prob_low = prob_rows.astype(jnp.bfloat16)
    context = jnp.dot(prob_low, values_all, preferred_element_type=jnp.float32)
    row_delta = jnp.sum(grad_here.astype(jnp.float32) * context, axis=1, keepdims=True)
    prob_grad = contract_cols(grad_here, values_all)
    score_grad = (prob_rows * (prob_grad - row_delta) * inv_root).astype(jnp.bfloat16)
    query_grad = jnp.dot(score_grad, keys_all, preferred_element_type=jnp.float32).astype(
        jnp.bfloat16
    )
    key_terms = contract_rows(score_grad, query_here)
    value_terms = contract_rows(prob_low, grad_here)
    grad_terms = jnp.concatenate([key_terms, value_terms], axis=1).reshape(
        seq_count, tok_count, kv_width
    )
    received = lax.all_to_all(
        grad_terms.astype(jnp.bfloat16), "seq", split_axis=0, concat_axis=0, tiled=True
    ).astype(grad_terms.dtype)
    kv_grad = jnp.sum(received, axis=0).astype(jnp.bfloat16)
    grad_slice = lax.psum_scatter(
        contract_rows(tokens_here, kv_grad).astype(jnp.bfloat16),
        "seq",
        scatter_dimension=0,
        tiled=True,
    ).astype(jnp.float32)
    branches = [
        partial(gossip, distance=(1 << level_idx) % rep_count, rep_count=rep_count)
        for level_idx in range(4)
    ]
    mixed_update = lax.switch(step_count[0] % 4, branches, grad_slice)
    return (mixed_update[None], query_grad[None])


def solution(mesh):
    return jax.shard_map(
        per_device,
        mesh=mesh,
        in_specs=(
            P("rep", "seq", None),
            P("rep", "seq", None),
            P("rep", "seq", None),
            P("rep", "seq", None),
            P(),
            P(),
        ),
        out_specs=(P("rep", "seq", None), P("rep", "seq", None)),
        check_vma=False,
    )
```

profile of v0, /device:TPU:8, one launch (start us, length us, event | category | flops | bytes accessed | tf_op | source)
XLA Modules:
  0.0 498.9 jit_solution(13018875669005355405)
XLA Ops:
  7.2 0.7 all-gather.6.cloned.1.call-update
  8.0 114.0 %all-gather.6.cloned.1.call-done = bf16[1,6144,256]{2,1,0:T(8,128)(2,1)} async-done(((bf16[1,384,256]{2,1,0:T(8,128)(2,1)}), bf16[1,6144,256]{2,1,0:T(8,128)(2,1)}) %all-gather.6.cloned.1.call-update) | async-done | bytes 3145744 | tf_op jit(solution)/shard_map/all_gather | solution.py:78
  121.9 3.5 fusion.13
  126.3 82.9 %all-gather.4.cloned.1.call-done = bf16[4096,256]{1,0:T(8,128)(2,1)} async-done(((bf16[256,256]{1,0:T(8,128)(2,1)}), bf16[4096,256]{1,0:T(8,128)(2,1)}) %all-gather.4.cloned.1.call-update) | async-done | bytes 2097168 | tf_op jit(solution)/shard_map/all_gather | solution.py:81
  209.2 0.3 broadcast_in_dim.34
  209.5 2.4 fusion.31
  211.9 0.3 fusion.12
  212.2 0.8 convolution_convert_fusion.1
  213.0 0.8 copy-done.2
  213.8 0.6 fusion.18
  214.4 0.8 fusion.7
  215.2 0.8 convolution_convert_fusion.2
  216.0 0.2 pad_maximum_fusion
  216.2 0.3 copy-done.1
  216.5 0.2 copy.35
  216.7 50.3 %all_to_all.5 = bf16[16,256,256]{1,2,0:T(8,128)(2,1)} all-to-all(bf16[16,256,256]{1,2,0:T(8,128)(2,1)S(1)} %bitcast.69), channel_id=1, replica_groups=mesh['rep'=32,'seq'=16] {'seq'}, dimensions={0} | all-to-all | bytes 4194304 | tf_op jit(solution)/shard_map/all_to_all | solution.py:105
  267.0 1.9 reduce_sum.32
  268.9 2.7 fusion
  271.5 4.6 copy.30
  276.9 3.2 fusion.19
  280.1 184.1 %reduce-scatter.4.cloned.1.call-done = bf16[384,256]{1,0:T(8,128)(2,1)} async-done(((bf16[6144,256]{1,0:T(8,128)(2,1)}), bf16[384,256]{1,0:T(8,128)(2,1)}) %reduce-scatter.4.cloned.1.call-update) | async-done | bytes 196624
  464.2 1.7 copy.31
  466.0 1.0 convert_element_type.89
  466.9 24.7 %conditional.1 = (f32[1,384,256]{2,1,0:T(8,128)S(1)}) conditional(s32[]{:T(128)} %clamp.3, f32[384,256]{0,1:T(8,128)S(1)} %convert_element_type.89, f32[384,256]{0,1:T(8,128)S(1)} %convert_element_type.89, f32[384,256]{0,1:T(8,128)S(1)} %convert_element_type.89, f32[384,256]{0,1:T(8,128)S(1)} %convert_element_type.89), branch_computations={%region_5.6_spmd, %region_6.7_spmd, %region_7.8_spmd, %region_8.9_... | conditional | flops 589824 | bytes 4128856 | solution.py:119
  467.0 0.9 copy.27
  467.9 1.0 convert_element_type.64
  468.9 5.1 %collective-permute-start.3 = (bf16[384,256]{1,0:T(8,128)(2,1)S(1)}, bf16[384,256]{1,0:T(8,128)(2,1)S(1)}, u32[]{:S(2)}, u32[]{:S(2)}) collective-permute-start(bf16[384,256]{1,0:T(8,128)(2,1)S(1)} %convert_element_type.64), channel_id=1, source_target_pairs={{0,480},{16,496},{32,0},{48,16},{64,32},{80,48},{96,64},{112,80},{... | collective-permute-start | bytes 589832 | tf_op jit(solution)/shard_map/cond/branch_1_fun/ppermute | solution.py:21
  474.0 2.3 collective-permute-start.2
  476.3 1.7 collective-permute-done.3
  478.0 12.6 %collective-permute-done.2 = bf16[384,256]{1,0:T(8,128)(2,1)S(1)} collective-permute-done((bf16[384,256]{1,0:T(8,128)(2,1)S(1)}, bf16[384,256]{1,0:T(8,128)(2,1)S(1)}, u32[]{:S(2)}, u32[]{:S(2)}) %collective-permute-start.2) | collective-permute-done | bytes 196640 | tf_op jit(solution)/shard_map/cond/branch_1_fun/ppermute | solution.py:21
  490.6 1.1 multiply_bitcast_fusion.1
  491.7 0.7 copy-done.3
  (25 shorter events, 0.9 us)
Async XLA Ops:
  7.2 114.8 %copy-start = (bf16[1,256,6144]{2,1,0:T(8,128)(2,1)S(1)}, bf16[1,256,6144]{2,1,0:T(8,128)(2,1)}, u32[]{:S(2)}) copy-start(bf16[1,256,6144]{2,1,0:T(8,128)(2,1)} %param.10) | copy-start | bytes 9437188
  7.2 114.8 %all-gather.6.cloned.1.call-start = ((), (), s32[]{:S(2)}) async-start(), calls=%async_computation.3 | async-start | bytes 3342336 | tf_op jit(solution)/shard_map/all_gather | solution.py:78
  7.9 117.7 %copy-start.6 = (s32[64,3]{0,1:T(4,128)S(1)}, s32[64,3]{0,1:T(4,128)}, u32[]{:S(2)}) copy-start(s32[64,3]{0,1:T(4,128)} %param.14) | copy-start | bytes 2308
  7.9 118.3 %copy-start.5 = (bf16[1,256,128]{2,1,0:T(8,128)(2,1)S(1)}, bf16[1,256,128]{2,1,0:T(8,128)(2,1)}, u32[]{:S(2)}) copy-start(bf16[1,256,128]{2,1,0:T(8,128)(2,1)} %param.12) | copy-start | bytes 196612
  7.9 201.5 %copy-start.4 = (bf16[1,256,128]{2,1,0:T(8,128)(2,1)S(1)}, bf16[1,256,128]{2,1,0:T(8,128)(2,1)}, u32[]{:S(2)}) copy-start(bf16[1,256,128]{2,1,0:T(8,128)(2,1)} %param.11) | copy-start | bytes 196612
  7.9 201.2 %all-gather.4.cloned.1.call-start = ((), (), s32[]{:S(2)}) async-start(), calls=%async_computation.2 | async-start | bytes 2228224 | tf_op jit(solution)/shard_map/all_gather | solution.py:81
  125.5 338.7 %reduce-scatter.4.cloned.1.call-start = ((), (), s32[]{:S(2)}) async-start(), calls=%async_computation.4 | async-start | bytes 3342336
  212.2 1.6 copy-start.2
  215.2 1.4 copy-start.1
  468.9 9.1 %collective-permute-start.3 = (bf16[384,256]{1,0:T(8,128)(2,1)S(1)}, bf16[384,256]{1,0:T(8,128)(2,1)S(1)}, u32[]{:S(2)}, u32[]{:S(2)}) collective-permute-start(bf16[384,256]{1,0:T(8,128)(2,1)S(1)} %convert_element_type.64), channel_id=1, source_target_pairs={{0,480},{16,496},{32,0},{48,16},{64,32},{80,48},{96,64},{112,80},{... | collective-permute-start | bytes 589832 | tf_op jit(solution)/shard_map/cond/branch_1_fun/ppermute | solution.py:21
  474.0 16.6 %collective-permute-start.2 = (bf16[384,256]{1,0:T(8,128)(2,1)S(1)}, bf16[384,256]{1,0:T(8,128)(2,1)S(1)}, u32[]{:S(2)}, u32[]{:S(2)}) collective-permute-start(bf16[384,256]{1,0:T(8,128)(2,1)S(1)} %convert_element_type.64), channel_id=1, source_target_pairs={{0,32},{16,48},{32,64},{48,80},{64,96},{80,112},{96,128},{112,144}... | collective-permute-start | bytes 589832 | tf_op jit(solution)/shard_map/cond/branch_1_fun/ppermute | solution.py:21
  491.7 0.7 copy-start.3
Sparse Core Ops, SparseCore 0:
  11.3 110.5 all-gather.5
  125.8 83.3 all-gather.3
  276.3 187.8 reduce-scatter.3
where the time goes:
time: 499 us
  waiting for transfers between devices  396 us (79%)
  blocking collectives  50.3 us (10%)
  matrix products  14.8 us (3%)
  between operations  14.6 us (3%)
  local copies, waits for them, and re-layouts  10.2 us (2%)
  starting transfers between devices  7.46 us (1%)
  other arithmetic  5.65 us (1%)
    unnamed x4, waiting for transfers between devices  185 us
    all_gather x1, waiting for transfers between devices, per_device(): lax.all_gather(weight_here, 'seq', axis=0, tiled=True)  114 us
    all_gather x1, waiting for transfers between devices, per_device(): kv_all = lax.all_gather(kv_here, 'seq', axis=0, tiled=True)  82.9 us
    all_to_all x1, blocking collectives, per_device(): lax.all_to_all(grad_terms.astype(jnp.bfloat16), 'seq', split_axis=0, conc...  50.3 us
    ppermute x2, waiting for transfers between devices, shifted(): return lax.ppermute(value, axis, pairs)  14.3 us
  transfers between devices with their start and end apart: 5, of which 5 were waited for; matrix products, arithmetic and copies ran while one was open for 1% of the time, Pallas kernels for 0%

commit v1 on v0

--- a/solution.py
+++ b/solution.py
@@ -5,6 +5,15 @@
 from jax.sharding import PartitionSpec as P
 
 BLOCK = 64
+handle_pieces_all = lambda w_in, dim_no: jnp.concatenate(
+    jax.lax.all_to_all(
+        jnp.stack([w_in] * jax.lax.axis_size("seq"), 0),
+        axis_name="seq",
+        split_axis=0,
+        concat_axis=0,
+    ),
+    dim_no,
+)
 
 
 def for_sending(value):
@@ -75,9 +84,7 @@
     blocks_dev = tok_count // blk_size
     block_count = blocks_dev * seq_count
     inv_root = head_size ** (-0.5)
-    kv_here = fold_rows(tokens_here, lax.all_gather(weight_here, "seq", axis=0, tiled=True)).astype(
-        jnp.bfloat16
-    )
+    kv_here = fold_rows(tokens_here, handle_pieces_all(weight_here, 0)).astype(jnp.bfloat16)
     kv_all = lax.all_gather(kv_here, "seq", axis=0, tiled=True)
     keys_all = kv_all[:, :head_size]
     values_all = kv_all[:, head_size:]

time: 499 us -> 551 us (1.10)
  blocking collectives: 50.3 us -> 138 us
  waiting for transfers between devices: 396 us -> 360 us
    all_gather x1 -> x0, waiting for transfers between devices: 114 us -> none  [per_device(): lax.all_gather(weight_here, 'seq', axis=0, tiled=True)]
    all_to_all x0 -> x1, blocking collectives: none -> 87.7 us  [jax.lax.all_to_all(jnp.stack([w_in] * jax.lax.axis_size('seq'), 0), axis_...]
    all_gather x1, waiting for transfers between devices: 82.9 us -> 161 us  [per_device(): kv_all = lax.all_gather(kv_here, 'seq', axis=0, tiled=True)]
    unnamed x4 -> x3, waiting for transfers between devices: 185 us -> 184 us
  transfers between devices with their start and end apart: 5 -> 4, of which waited for: 5 -> 4; matrix products, arithmetic and copies ran while one was open for 1% -> 1% of each run, Pallas kernels for 0% -> 0%
where the time goes in v1:
time: 551 us; the launch traced here: 550 us
  waiting for transfers between devices  360 us (65%)
  blocking collectives  138 us (25%)
  between operations  14.9 us (3%)
  matrix products  12.9 us (2%)
  local copies, waits for them, and re-layouts  11.5 us (2%)
  starting transfers between devices  7.43 us (1%)
  other arithmetic  5.65 us (1%)
    unnamed x3, waiting for transfers between devices  184 us
    all_gather x1, waiting for transfers between devices, per_device(): kv_all = lax.all_gather(kv_here, 'seq', axis=0, tiled=True)  161 us
    all_to_all x1, blocking collectives, jax.lax.all_to_all(jnp.stack([w_in] * jax.lax.axis_size('seq'), 0), axis_...  87.7 us
    all_to_all x1, blocking collectives, per_device(): lax.all_to_all(grad_terms.astype(jnp.bfloat16), 'seq', split_axis=0, conc...  50.4 us
    ppermute x2, waiting for transfers between devices, shifted(): return lax.ppermute(value, axis, pairs)  14.3 us
  transfers between devices with their start and end apart: 4, of which 4 were waited for; matrix products, arithmetic and copies ran while one was open for 1% of the time, Pallas kernels for 0%

profile of v1, /device:TPU:8, one launch (start us, length us, event | category | flops | bytes accessed | tf_op | source)
XLA Modules:
  0.0 550.4 jit_solution(17984893096840618144)
XLA Ops:
  7.2 1.4 stack.3
  8.6 87.7 %all_to_all.10 = bf16[16,384,256]{2,1,0:T(8,128)(2,1)S(1)} all-to-all(bf16[16,384,256]{2,1,0:T(8,128)(2,1)S(1)} %stack.3), channel_id=1, replica_groups=mesh['rep'=32,'seq'=16] {'seq'}, dimensions={0} | all-to-all | bytes 6291456 | tf_op jit(solution)/shard_map/all_to_all | solution.py:9
  96.3 1.7 fusion.12
  98.9 161.5 %all-gather.2.cloned.1.call-done = bf16[4096,256]{1,0:T(8,128)(2,1)} async-done(((bf16[256,256]{1,0:T(8,128)(2,1)}), bf16[4096,256]{1,0:T(8,128)(2,1)}) %all-gather.2.cloned.1.call-update) | async-done | bytes 2097168 | tf_op jit(solution)/shard_map/all_gather | solution.py:88
  260.3 0.3 broadcast_in_dim.34
  260.6 2.4 fusion.28
  263.0 0.3 fusion.11
  263.4 0.8 convolution_convert_fusion.1
  264.2 0.8 copy-done.2
  264.9 0.6 fusion.15
  265.5 0.8 fusion.7
  266.3 0.8 convolution_convert_fusion.2
  267.1 0.2 pad_maximum_fusion
  267.3 0.3 copy-done.1
  267.7 0.2 copy.35
  267.9 50.4 %all_to_all.11 = bf16[16,256,256]{1,2,0:T(8,128)(2,1)} all-to-all(bf16[16,256,256]{1,2,0:T(8,128)(2,1)S(1)} %bitcast.67), channel_id=1, replica_groups=mesh['rep'=32,'seq'=16] {'seq'}, dimensions={0} | all-to-all | bytes 4194304 | tf_op jit(solution)/shard_map/all_to_all | solution.py:112
  318.3 1.9 reduce_sum.32
  320.2 2.7 fusion
  322.9 4.6 copy.30
  328.2 3.2 fusion.16
  331.4 184.0 %reduce-scatter.4.cloned.1.call-done = bf16[384,256]{1,0:T(8,128)(2,1)} async-done(((bf16[6144,256]{1,0:T(8,128)(2,1)}), bf16[384,256]{1,0:T(8,128)(2,1)}) %reduce-scatter.4.cloned.1.call-update) | async-done | bytes 196624
  515.4 1.7 copy.31
  517.1 1.0 convert_element_type.89
  518.1 24.7 %conditional.1 = (f32[1,384,256]{2,1,0:T(8,128)S(1)}) conditional(s32[]{:T(128)} %clamp.3, f32[384,256]{0,1:T(8,128)S(1)} %convert_element_type.89, f32[384,256]{0,1:T(8,128)S(1)} %convert_element_type.89, f32[384,256]{0,1:T(8,128)S(1)} %convert_element_type.89, f32[384,256]{0,1:T(8,128)S(1)} %convert_element_type.89), branch_computations={%region_5.6_spmd, %region_6.7_spmd, %region_7.8_spmd, %region_8.9_... | conditional | flops 589824 | bytes 4128856 | solution.py:126
  518.1 0.9 copy.27
  519.0 1.0 convert_element_type.64
  520.1 5.0 collective-permute-start.3
  525.1 2.3 collective-permute-start.2
  527.4 1.7 collective-permute-done.3
  529.1 12.6 %collective-permute-done.2 = bf16[384,256]{1,0:T(8,128)(2,1)S(1)} collective-permute-done((bf16[384,256]{1,0:T(8,128)(2,1)S(1)}, bf16[384,256]{1,0:T(8,128)(2,1)S(1)}, u32[]{:S(2)}, u32[]{:S(2)}) %collective-permute-start.2) | collective-permute-done | bytes 196640 | tf_op jit(solution)/shard_map/cond/branch_1_fun/ppermute | solution.py:30
  541.7 1.1 multiply_bitcast_fusion.1
  542.8 0.7 copy-done.3
  (24 shorter events, 0.9 us)
Async XLA Ops:
  7.2 89.2 %copy-start = (bf16[1,256,6144]{2,1,0:T(8,128)(2,1)S(1)}, bf16[1,256,6144]{2,1,0:T(8,128)(2,1)}, u32[]{:S(2)}) copy-start(bf16[1,256,6144]{2,1,0:T(8,128)(2,1)} %param.10) | copy-start | bytes 9437188
  7.2 253.1 %all-gather.2.cloned.1.call-start = ((), (), s32[]{:S(2)}) async-start(), calls=%async_computation.3 | async-start | bytes 2228224 | tf_op jit(solution)/shard_map/all_gather | solution.py:88
  96.3 1.8 copy-start.6
  96.3 2.4 copy-start.5
  96.3 164.3 %copy-start.4 = (bf16[1,256,128]{2,1,0:T(8,128)(2,1)S(1)}, bf16[1,256,128]{2,1,0:T(8,128)(2,1)}, u32[]{:S(2)}) copy-start(bf16[1,256,128]{2,1,0:T(8,128)(2,1)} %param.11) | copy-start | bytes 196612
  98.0 417.4 %reduce-scatter.4.cloned.1.call-start = ((), (), s32[]{:S(2)}) async-start(), calls=%async_computation.4 | async-start | bytes 3342336
  263.3 1.6 copy-start.2
  266.3 1.4 copy-start.1
  520.1 9.1 %collective-permute-start.3 = (bf16[384,256]{1,0:T(8,128)(2,1)S(1)}, bf16[384,256]{1,0:T(8,128)(2,1)S(1)}, u32[]{:S(2)}, u32[]{:S(2)}) collective-permute-start(bf16[384,256]{1,0:T(8,128)(2,1)S(1)} %convert_element_type.64), channel_id=1, source_target_pairs={{0,480},{16,496},{32,0},{48,16},{64,32},{80,48},{96,64},{112,80},{... | collective-permute-start | bytes 589832 | tf_op jit(solution)/shard_map/cond/branch_1_fun/ppermute | solution.py:30
  525.1 16.6 %collective-permute-start.2 = (bf16[384,256]{1,0:T(8,128)(2,1)S(1)}, bf16[384,256]{1,0:T(8,128)(2,1)S(1)}, u32[]{:S(2)}, u32[]{:S(2)}) collective-permute-start(bf16[384,256]{1,0:T(8,128)(2,1)S(1)} %convert_element_type.64), channel_id=1, source_target_pairs={{0,32},{16,48},{32,64},{48,80},{64,96},{80,112},{96,128},{112,144}... | collective-permute-start | bytes 589832 | tf_op jit(solution)/shard_map/cond/branch_1_fun/ppermute | solution.py:30
  542.8 0.7 copy-start.3
Sparse Core Ops, SparseCore 0:
  98.1 162.1 all-gather.1
  327.6 187.7 reduce-scatter.3
